TPU v7x, 32 devices: a whole 2x2x4 slice. The times are simulated.
32 devices in a mesh: outer: 4 (over y, core), inner: 8 (over z, x).
Axes of the slice: x: 2, y: 2, z: 4, core: 2. Of those that a mesh axis runs over, the one named last changes fastest.
Arguments:
- queries: bfloat16 [4, 8, 8, 64, 512], P('outer', None, 'inner'), may hold values from -240 to 240
- keys: bfloat16 [4, 8, 8, 64, 128], P('outer', None, 'inner'), may hold values from -6 to 6
- values: bfloat16 [4, 8, 8, 64, 128], P('outer', None, 'inner'), may hold values from -6 to 6
- grad_out: bfloat16 [4, 8, 8, 64, 512], P('outer', None, 'inner'), may hold values from -6 to 6
- doc_starts: int32 [4, 8, 4], replicated, may hold values from 0 to 512, as said below
Outputs:
- attn_out: bfloat16 [4, 8, 8, 64, 512], P('outer', None, 'inner')
- query_grads: bfloat16 [4, 8, 8, 64, 512], P('outer', None, 'inner')
- key_grads: bfloat16 [4, 8, 8, 64, 128], P('outer', None, 'inner')
- value_grads: bfloat16 [4, 8, 8, 64, 128], P('outer', None, 'inner')
Inputs may be any that keep to these rules, and one draw needn't show every extreme that they name: `doc_starts`: entry [o, u, j] is an offset within unit u of segment o at which a document starts, or 512 for none. The offsets below 512 of a unit are distinct, rise with j and stand before all its 512 entries. Offset 0 starts a document in every even unit except unit 0 of segments o > 0; unit 0 of such a segment and an odd unit may continue the document of the position before them (then their first entry is not 0). The last unit of every segment continues the one before it; position 0 of the sequence starts a document.
All inputs are finite; a program needn't handle non-finite values.
Results may differ from a plain program's by a relative error of at most 0.0075.
Values may be sent and summed in bfloat16 or wider, within the bound.
No kernel may reach another device: no remote copies, remote signals or barrier semaphores. Data moves between devices by JAX's collectives and lax.ppermute only.
A program may use at most 128 MiB of HBM per device.

v0:
```python
import math
import jax
import jax.numpy as jnp
from jax import lax
from jax.sharding import PartitionSpec as P


def passed_along(x, axis, by):
    size = lax.axis_size(axis)
    pairs = [(i, i + by) for i in range(size) if 0 <= i + by < size]
    return lax.ppermute(x, axis, pairs)


def doc_table(doc_starts, tok_dev):
    n_outer, n_inner, n_slots = doc_starts.shape
    flat_starts = doc_starts.reshape(n_outer * n_inner, n_slots)
    start_counts = jnp.sum((flat_starts < tok_dev).astype(jnp.int32), axis=1)
    first_index = jnp.cumsum(start_counts) - start_counts
    offsets = jnp.arange(tok_dev, dtype=jnp.int32)
    inside_count = jnp.sum(
        (flat_starts[:, None, :] <= offsets[None, :, None]).astype(jnp.int32), axis=2
    )
    return (first_index[:, None] + inside_count - 1).reshape(n_outer, n_inner, tok_dev)


def owner_table(doc_starts):
    n_outer, n_inner = (doc_starts.shape[0], doc_starts.shape[1])
    pairs = n_inner // 2
    joined = (doc_starts[:, 1::2, 0] != 0).astype(jnp.int32)
    pair_ids = jnp.arange(pairs, dtype=jnp.int32)
    relative = jnp.where(pair_ids == 0, 0, jnp.where(pair_ids == pairs - 1, 1, pair_ids + 1))
    pair_owner = (jnp.arange(n_outer, dtype=jnp.int32)[:, None] + relative[None, :]) % pairs
    even_owner = 2 * pair_owner
    owner = jnp.stack([even_owner, even_owner + 1 - joined], axis=2)
    return owner.reshape(n_outer, n_inner)


def slot_table(unit_owner):
    n_inner = unit_owner.shape[1]
    same_owner = unit_owner[:, :, None] == unit_owner[:, None, :]
    earlier = jnp.arange(n_inner)[None, :] < jnp.arange(n_inner)[:, None]
    return jnp.sum((same_owner & earlier[None]).astype(jnp.int32), axis=2)


def route_table(target_row, slot_row, slot_count):
    n_units = target_row.shape[0]
    unit_ids = jnp.arange(n_units, dtype=jnp.int32)
    tables = []
    for slot_id in range(slot_count):
        matched = (target_row[None, :] == unit_ids[:, None]) & (slot_row[None, :] == slot_id)
        present = jnp.any(matched, axis=1)
        chosen = jnp.sum(jnp.where(matched, unit_ids[None, :], 0), axis=1)
        tables.append(jnp.where(present, chosen, n_units))
    return jnp.stack(tables)


def pack_rows(piece_rows, index_table):
    padded = jnp.concatenate(
        [piece_rows, jnp.zeros((1,) + piece_rows.shape[1:], piece_rows.dtype)], axis=0
    )
    return padded[index_table]


def unpack(arrived, target_row, slot_row):
    n_slots, n_inner = (arrived.shape[0], arrived.shape[1])
    flat_rows = arrived.reshape((n_slots * n_inner,) + arrived.shape[2:])
    return flat_rows[slot_row * n_inner + target_row]


def holder_meta(owner_row, slot_row, docs_row, holder, seg_start, is_valid, missing):
    n_inner, tok_dev = docs_row.shape
    unit_ids = jnp.arange(n_inner, dtype=jnp.int32)
    offsets = jnp.arange(tok_dev, dtype=jnp.int32)
    places, labels = ([], [])
    for slot_id in range(2):
        matched = (owner_row == holder) & (slot_row == slot_id)
        unit_id = jnp.sum(jnp.where(matched, unit_ids, 0))
        present = jnp.any(matched) & is_valid
        places.append(seg_start + unit_id * tok_dev + offsets)
        labels.append(jnp.where(present, docs_row[unit_id], missing))
    return (jnp.concatenate(places), jnp.concatenate(labels))


def attend(
    query_buf, grad_buf, query_pos, query_doc, key_buf, value_buf, key_pos, key_doc, n_heads
):
    n_rows = query_buf.shape[0]
    head_dim = key_buf.shape[1]
    scaling = 1.0 / math.sqrt(head_dim)
    q_three = query_buf.reshape(n_rows, n_heads, head_dim)
    g_three = grad_buf.reshape(n_rows, n_heads, head_dim)
    scores = (
        jnp.einsum("qhd,kd->hqk", q_three, key_buf, preferred_element_type=jnp.float32) * scaling
    )
    allowed = (query_doc[:, None] == key_doc[None, :]) & (key_pos[None, :] <= query_pos[:, None])
    scores = jnp.where(allowed[None], scores, -jnp.inf)
    row_max = jnp.max(scores, axis=2, keepdims=True)
    log_total = row_max + jnp.log(jnp.sum(jnp.exp(scores - row_max), axis=2, keepdims=True))
    probs = jnp.exp(scores - log_total)
    probs_low = probs.astype(jnp.bfloat16)
    attn = jnp.einsum(
        "hqk,kd->qhd", probs_low, value_buf, preferred_element_type=jnp.float32
    ).astype(jnp.bfloat16)
    inner_prod = jnp.sum(g_three.astype(jnp.float32) * attn.astype(jnp.float32), axis=2)
    grad_probs = jnp.einsum("qhd,kd->hqk", g_three, value_buf, preferred_element_type=jnp.float32)
    score_grads = (probs * (grad_probs - inner_prod.T[:, :, None])).astype(jnp.bfloat16)
    q_grads = (
        jnp.einsum("hqk,kd->qhd", score_grads, key_buf, preferred_element_type=jnp.float32)
        * scaling
    )
    k_grads = (
        jnp.einsum("hqk,qhd->kd", score_grads, q_three, preferred_element_type=jnp.float32)
        * scaling
    )
    v_grads = jnp.einsum("hqk,qhd->kd", probs_low, g_three, preferred_element_type=jnp.float32)
    return (
        attn.reshape(n_rows, -1),
        q_grads.astype(jnp.bfloat16).reshape(n_rows, -1),
        k_grads,
        v_grads,
    )


def shards(queries, keys, values, grad_out, doc_starts):
    n_inner = lax.axis_size("inner")
    piece_len = queries.shape[3]
    width_q = queries.shape[4]
    head_dim = keys.shape[4]
    n_heads = width_q // head_dim
    tok_dev = piece_len * n_inner
    seg_len = tok_dev * n_inner
    outer_id = lax.axis_index("outer")
    inner_id = lax.axis_index("inner")
    unit_owner = owner_table(doc_starts)
    slot_all = slot_table(unit_owner)
    docs_all = doc_table(doc_starts, tok_dev)
    own_owner = unit_owner[outer_id]
    own_slot = slot_all[outer_id]
    own_docs = docs_all[outer_id]
    before = jnp.maximum(outer_id - 1, 0)
    prev_owner = unit_owner[before]
    prev_slot = slot_all[before]
    prev_docs = docs_all[before]
    has_before = outer_id > 0
    seg_start = outer_id * seg_len
    prev_start = before * seg_len
    query_rows = queries[0, :, 0]
    key_rows = keys[0, :, 0]
    value_rows = values[0, :, 0]
    grad_rows = grad_out[0, :, 0]
    hold_index = route_table(own_owner, own_slot, 2)
    q_in, k_in, v_in, g_in = (
        lax.all_to_all(
            pack_rows(query_rows, hold_index), "inner", split_axis=1, concat_axis=1, tiled=True
        ),
        lax.all_to_all(
            pack_rows(key_rows, hold_index), "inner", split_axis=1, concat_axis=1, tiled=True
        ),
        lax.all_to_all(
            pack_rows(value_rows, hold_index), "inner", split_axis=1, concat_axis=1, tiled=True
        ),
        lax.all_to_all(
            pack_rows(grad_rows, hold_index), "inner", split_axis=1, concat_axis=1, tiled=True
        ),
    )
    query_buf = q_in.reshape(2 * tok_dev, width_q)
    grad_buf = g_in.reshape(2 * tok_dev, width_q)
    key_buf = k_in.reshape(2 * tok_dev, head_dim)
    value_buf = v_in.reshape(2 * tok_dev, head_dim)
    prev_keys, prev_values = passed_along((key_buf, value_buf), "outer", 1)
    query_pos, query_doc = holder_meta(
        own_owner, own_slot, own_docs, inner_id, seg_start, outer_id >= 0, -1
    )
    ctx_keys = jnp.concatenate([key_buf, prev_keys])
    ctx_values = jnp.concatenate([value_buf, prev_values])
    own_pos, own_doc = holder_meta(
        own_owner, own_slot, own_docs, inner_id, seg_start, outer_id >= 0, -1
    )
    back_pos, back_doc = holder_meta(
        prev_owner, prev_slot, prev_docs, inner_id, prev_start, has_before, -2
    )
    key_pos = jnp.concatenate([own_pos, back_pos])
    key_doc = jnp.concatenate([own_doc, back_doc])
    attn, q_grads, k_grads, v_grads = attend(
        query_buf, grad_buf, query_pos, query_doc, ctx_keys, ctx_values, key_pos, key_doc, n_heads
    )
    later_kg, later_vg = passed_along((k_grads[2 * tok_dev :], v_grads[2 * tok_dev :]), "outer", -1)
    key_total = (
        (k_grads[: 2 * tok_dev] + later_kg)
        .astype(jnp.bfloat16)
        .reshape(2, n_inner, piece_len, head_dim)
    )
    value_total = (
        (v_grads[: 2 * tok_dev] + later_vg)
        .astype(jnp.bfloat16)
        .reshape(2, n_inner, piece_len, head_dim)
    )
    attn_back, qg_back, kg_back, vg_back = (
        lax.all_to_all(
            attn.reshape(2, n_inner, piece_len, width_q),
            "inner",
            split_axis=1,
            concat_axis=1,
            tiled=True,
        ),
        lax.all_to_all(
            q_grads.reshape(2, n_inner, piece_len, width_q),
            "inner",
            split_axis=1,
            concat_axis=1,
            tiled=True,
        ),
        lax.all_to_all(key_total, "inner", split_axis=1, concat_axis=1, tiled=True),
        lax.all_to_all(value_total, "inner", split_axis=1, concat_axis=1, tiled=True),
    )
    attn_rows = unpack(attn_back, own_owner, own_slot)
    qgrad_rows = unpack(qg_back, own_owner, own_slot)
    kgrad_rows = unpack(kg_back, own_owner, own_slot)
    vgrad_rows = unpack(vg_back, own_owner, own_slot)
    shape_q = (1, n_inner, 1, piece_len, width_q)
    shape_k = (1, n_inner, 1, piece_len, head_dim)
    return (
        attn_rows.reshape(shape_q),
        qgrad_rows.reshape(shape_q),
        kgrad_rows.reshape(shape_k),
        vgrad_rows.reshape(shape_k),
    )


def solution(mesh):
    return jax.shard_map(
        shards,
        mesh=mesh,
        in_specs=(
            P("outer", None, "inner", None, None),
            P("outer", None, "inner", None, None),
            P("outer", None, "inner", None, None),
            P("outer", None, "inner", None, None),
            P(),
        ),
        out_specs=(
            P("outer", None, "inner", None, None),
            P("outer", None, "inner", None, None),
            P("outer", None, "inner", None, None),
            P("outer", None, "inner", None, None),
        ),
        check_vma=False,
    )
```

profile of v0, /device:TPU:0, one launch (start us, length us, event | category | flops | bytes accessed | tf_op | source)
XLA Modules:
  0.0 296.2 jit_solution(16554586157267958369)
XLA Ops:
  5.2 7.3 %all-to-all-start.1 = ((bf16[2,8,64,128]{3,2,0,1:T(8,128)(2,1)}), bf16[2,8,64,128]{3,2,0,1:T(8,128)(2,1)S(1)}, u32[]{:S(2)}, u32[]{:S(2)}) async-start(bf16[2,8,64,128]{3,2,0,1:T(8,128)(2,1)} %copy.125), calls=%async_computation.1 | async-start | bytes 524288 | tf_op jit(solution)/shard_map/all_to_all | solution.py:156
  14.8 6.7 %all-to-all-done.1 = bf16[2,8,64,128]{3,2,0,1:T(8,128)(2,1)S(1)} async-done(((bf16[2,8,64,128]{3,2,0,1:T(8,128)(2,1)}), bf16[2,8,64,128]{3,2,0,1:T(8,128)(2,1)S(1)}, u32[]{:S(2)}, u32[]{:S(2)}) %all-to-all-start.1) | async-done | bytes 262176 | tf_op jit(solution)/shard_map/all_to_all | solution.py:156
  21.4 3.6 %all-to-all-start = ((bf16[2,8,64,128]{3,2,0,1:T(8,128)(2,1)}), bf16[2,8,64,128]{3,2,0,1:T(8,128)(2,1)S(1)}, u32[]{:S(2)}, u32[]{:S(2)}) async-start(bf16[2,8,64,128]{3,2,0,1:T(8,128)(2,1)} %copy.118), calls=%async_computation | async-start | bytes 524288 | tf_op jit(solution)/shard_map/all_to_all | solution.py:159
  27.9 5.7 %all-to-all-done = bf16[2,8,64,128]{3,2,0,1:T(8,128)(2,1)S(1)} async-done(((bf16[2,8,64,128]{3,2,0,1:T(8,128)(2,1)}), bf16[2,8,64,128]{3,2,0,1:T(8,128)(2,1)S(1)}, u32[]{:S(2)}, u32[]{:S(2)}) %all-to-all-start) | async-done | bytes 262176 | tf_op jit(solution)/shard_map/all_to_all | solution.py:159
  33.6 3.6 %all-to-all-start.2 = ((bf16[2,8,64,512]{3,2,0,1:T(8,128)(2,1)}), bf16[2,8,64,512]{3,2,0,1:T(8,128)(2,1)S(1)}, u32[]{:S(2)}, u32[]{:S(2)}) async-start(bf16[2,8,64,512]{3,2,0,1:T(8,128)(2,1)} %copy.127), calls=%async_computation.2 | async-start | bytes 2097152 | tf_op jit(solution)/shard_map/all_to_all | solution.py:153
  42.0 20.7 %all-to-all-done.2 = bf16[2,8,64,512]{3,2,0,1:T(8,128)(2,1)S(1)} async-done(((bf16[2,8,64,512]{3,2,0,1:T(8,128)(2,1)}), bf16[2,8,64,512]{3,2,0,1:T(8,128)(2,1)S(1)}, u32[]{:S(2)}, u32[]{:S(2)}) %all-to-all-start.2) | async-done | bytes 1048608 | tf_op jit(solution)/shard_map/all_to_all | solution.py:153
  62.7 3.6 %all-to-all-start.4 = ((bf16[2,8,64,512]{3,2,0,1:T(8,128)(2,1)}), bf16[2,8,64,512]{3,2,0,1:T(8,128)(2,1)S(1)}, u32[]{:S(2)}, u32[]{:S(2)}) async-start(bf16[2,8,64,512]{3,2,0,1:T(8,128)(2,1)} %copy.134), calls=%async_computation.4 | async-start | bytes 2097152 | tf_op jit(solution)/shard_map/all_to_all | solution.py:162
  89.9 4.0 %collective-permute-start = (bf16[1024,128]{0,1:T(8,128)(2,1)}, bf16[1024,128]{0,1:T(8,128)(2,1)}, u32[]{:S(2)}, u32[]{:S(2)}) collective-permute-start(bf16[1024,128]{0,1:T(8,128)(2,1)} %copy.121), channel_id=1, source_target_pairs={{0,8},{8,16},{16,24},{1,9},{9,17},{17,25},{2,10},{10,18},{18,26},{... | collective-permute-start | bytes 786440 | tf_op jit(solution)/shard_map/ppermute | solution.py:11
  101.3 3.2 %reshape.537 = bf16[1024,4,128]{0,2,1:T(8,128)(2,1)S(1)} reshape(bf16[2,8,64,512]{2,1,0,3:T(8,128)(2,1)} %copy.164) | data formatting | bytes 2097152 | tf_op jit(solution)/shard_map/reshape;reshape | solution.py:91
  104.5 15.2 %fusion.3 = (f32[4,1024]{1,0:T(4,128)S(1)}, f32[2048,1024,4]{1,0,2:T(8,128)}) fusion(pred[1024,2048]{0,1:T(8,128)(4,1)S(1)} %compare_and_fusion, bf16[1024,4,128]{2,1,0:T(4,128)(2,1)} %reshape_reshape.12, bf16[1024,128]{1,0:T(8,128)(2,1)} %collective-permute-done.1, bf16[1024,128]{1,0:T(8,128)(2,1)S(1)} %bitcast.128), kind=kOutput, calls=%fused_computation.15 | convolution fusion | flops 2173693952 | bytes 37240832 | tf_op jit(solution)/shard_map/qhd,kd->hqk/dot_general | solution.py:93
  119.8 14.3 %exponential_reduce_fusion = f32[4,1024]{1,0:T(4,128)S(1)} fusion(f32[2048,1024,4]{1,0,2:T(8,128)} %get-tuple-element.44, f32[4,1024]{1,0:T(4,128)S(1)} %get-tuple-element.43, pred[1024,2048]{0,1:T(8,128)(4,1)S(1)} %compare_and_fusion), kind=kLoop, calls=%fused_computation.13 | loop fusion | flops 33550336 | bytes 35684352 | tf_op jit(solution)/shard_map/reduce_sum | solution.py:98
  134.1 15.2 %convolution_bitcast_fusion = f32[2048,128]{1,0:T(8,128)} fusion(bf16[1024,4,128]{0,2,1:T(8,128)(2,1)S(1)} %reshape.537, f32[2048,1024,4]{1,0,2:T(8,128)} %get-tuple-element.44, f32[4,1024]{1,0:T(4,128)S(1)} %log_add_fusion, pred[1024,2048]{0,1:T(8,128)(4,1)S(1)} %compare_and_fusion), kind=kOutput, calls=%fused_computation.17 | convolution fusion | flops 2181038080 | bytes 37765120 | tf_op jit(solution)/shard_map/hqk,qhd->kd/dot_general | solution.py:115
  152.7 16.4 %multiply_reduce_fusion = (f32[1024,4]{0,1:T(4,128)S(1)}, bf16[1024,4,128]{0,2,1:T(8,128)(2,1)}) fusion(bf16[1024,4,128]{0,2,1:T(8,128)(2,1)S(1)} %reshape.537, f32[2048,1024,4]{1,0,2:T(8,128)} %get-tuple-element.44, f32[4,1024]{1,0:T(4,128)S(1)} %log_add_fusion, pred[1024,2048]{0,1:T(8,128)(4,1)S(1)} %compare_and_fusion, ...), kind=kOutput, calls=%fused_computation.21 | convolution fusion | flops 2184704000 | bytes 38305792 | tf_op jit(solution)/shard_map/hqk,kd->qhd/dot_general | solution.py:101
  169.1 16.5 %fusion.1 = bf16[4,1024,2048]{1,2,0:T(8,128)(2,1)S(1)} fusion(f32[2048,1024,4]{1,0,2:T(8,128)} %get-tuple-element.44, bf16[1024,4,128]{0,2,1:T(8,128)(2,1)} %copy-done.3, f32[4,1024]{1,0:T(4,128)S(1)} %bitcast.152, f32[4,1024]{1,0:T(4,128)S(1)} %log_add_fusion, pred[1024,2048]{0,1:T(8,128)(4,1)} %copy-done.1, bf16[1024,128]{0,1:T(8,128)(2,1)} %collective-permute-done, ...), kind=kOutput, calls=%fused_computation.10 | convolution fusion | flops 2198863872 | bytes 54034432 | tf_op jit(solution)/shard_map/qhd,kd->hqk/dot_general | solution.py:105
  185.6 5.7 %copy-done = bf16[4,1024,2048]{1,2,0:T(8,128)(2,1)} copy-done((bf16[4,1024,2048]{1,2,0:T(8,128)(2,1)}, bf16[4,1024,2048]{1,2,0:T(8,128)(2,1)S(1)}, u32[]{:S(2)}) %copy-start) | copy-done | bytes 16777240
  191.3 6.0 %fusion.4 = f32[2048,128]{1,0:T(8,128)S(1)} fusion(bf16[4,1024,2048]{1,2,0:T(8,128)(2,1)S(1)} %fusion.1, bf16[1024,4,128]{2,1,0:T(4,128)(2,1)} %reshape_reshape.12), kind=kOutput, calls=%fused_computation.19 | convolution fusion | flops 2147745792 | bytes 18874368 | tf_op jit(solution)/shard_map/hqk,qhd->kd/dot_general | solution.py:112
  200.6 5.9 %all-to-all-start.7 = ((bf16[2,8,64,128]{3,2,0,1:T(8,128)(2,1)}), bf16[2,8,64,128]{3,2,0,1:T(8,128)(2,1)S(1)}, u32[]{:S(2)}, u32[]{:S(2)}) async-start(bf16[2,8,64,128]{3,2,0,1:T(8,128)(2,1)} %copy.148), calls=%async_computation.7 | async-start | bytes 524288 | tf_op jit(solution)/shard_map/all_to_all | solution.py:214
  208.4 7.6 %all-to-all-done.7 = bf16[2,8,64,128]{3,2,0,1:T(8,128)(2,1)S(1)} async-done(((bf16[2,8,64,128]{3,2,0,1:T(8,128)(2,1)}), bf16[2,8,64,128]{3,2,0,1:T(8,128)(2,1)S(1)}, u32[]{:S(2)}, u32[]{:S(2)}) %all-to-all-start.7) | async-done | bytes 262176 | tf_op jit(solution)/shard_map/all_to_all | solution.py:214
  216.8 4.4 %all-to-all-start.6 = ((bf16[2,8,64,128]{3,2,0,1:T(8,128)(2,1)}), bf16[2,8,64,128]{3,2,0,1:T(8,128)(2,1)}, u32[]{:S(2)}, u32[]{:S(2)}) async-start(bf16[2,8,64,128]{3,2,0,1:T(8,128)(2,1)} %copy.145), calls=%async_computation.6 | async-start | bytes 524288 | tf_op jit(solution)/shard_map/all_to_all | solution.py:213
  221.1 8.3 %fusion.6 = bf16[1024,4,128]{0,2,1:T(8,128)(2,1)S(1)} fusion(bf16[4,1024,2048]{1,2,0:T(8,128)(2,1)} %copy-done, bf16[1024,128]{1,0:T(8,128)(2,1)} %collective-permute-done.1, bf16[1024,128]{1,0:T(8,128)(2,1)S(1)} %bitcast.129), kind=kOutput, calls=%fused_computation.24 | convolution fusion | flops 2149580800 | bytes 18350080 | tf_op jit(solution)/shard_map/hqk,kd->qhd/dot_general | solution.py:108
  233.3 6.0 %all-to-all-start.5 = ((bf16[2,8,64,512]{3,2,0,1:T(8,128)(2,1)}), bf16[2,8,64,512]{3,2,0,1:T(8,128)(2,1)S(1)}, u32[]{:S(2)}, u32[]{:S(2)}) async-start(bf16[2,8,64,512]{3,2,0,1:T(8,128)(2,1)} %copy.142), calls=%async_computation.5 | async-start | bytes 2097152 | tf_op jit(solution)/shard_map/all_to_all | solution.py:206
  244.7 20.4 %all-to-all-done.5 = bf16[2,8,64,512]{3,2,0,1:T(8,128)(2,1)S(1)} async-done(((bf16[2,8,64,512]{3,2,0,1:T(8,128)(2,1)}), bf16[2,8,64,512]{3,2,0,1:T(8,128)(2,1)S(1)}, u32[]{:S(2)}, u32[]{:S(2)}) %all-to-all-start.5) | async-done | bytes 1048608 | tf_op jit(solution)/shard_map/all_to_all | solution.py:206
  265.2 3.6 %all-to-all-start.3 = ((bf16[2,8,64,512]{3,2,0,1:T(8,128)(2,1)}), bf16[2,8,64,512]{3,2,0,1:T(8,128)(2,1)S(1)}, u32[]{:S(2)}, u32[]{:S(2)}) async-start(bf16[2,8,64,512]{3,2,0,1:T(8,128)(2,1)} %copy.132), calls=%async_computation.3 | async-start | bytes 2097152 | tf_op jit(solution)/shard_map/all_to_all | solution.py:199
  274.7 20.1 %all-to-all-done.3 = bf16[2,8,64,512]{3,2,0,1:T(8,128)(2,1)S(1)} async-done(((bf16[2,8,64,512]{3,2,0,1:T(8,128)(2,1)}), bf16[2,8,64,512]{3,2,0,1:T(8,128)(2,1)S(1)}, u32[]{:S(2)}, u32[]{:S(2)}) %all-to-all-start.3) | async-done | bytes 1048608 | tf_op jit(solution)/shard_map/all_to_all | solution.py:199
  (100 shorter events, 58.8 us)
Async XLA Ops:
  5.2 16.2 %all-to-all-start.1 = ((bf16[2,8,64,128]{3,2,0,1:T(8,128)(2,1)}), bf16[2,8,64,128]{3,2,0,1:T(8,128)(2,1)S(1)}, u32[]{:S(2)}, u32[]{:S(2)}) async-start(bf16[2,8,64,128]{3,2,0,1:T(8,128)(2,1)} %copy.125), calls=%async_computation.1 | async-start | bytes 524288 | tf_op jit(solution)/shard_map/all_to_all | solution.py:156
  21.4 3.6 %copy-start.5 = (bf16[2,8,64,128]{3,2,0,1:T(8,128)(2,1)}, bf16[2,8,64,128]{3,2,0,1:T(8,128)(2,1)S(1)}, u32[]{:S(2)}) copy-start(bf16[2,8,64,128]{3,2,0,1:T(8,128)(2,1)S(1)} %all-to-all-done.1) | copy-start | bytes 786436
  21.4 12.2 %all-to-all-start = ((bf16[2,8,64,128]{3,2,0,1:T(8,128)(2,1)}), bf16[2,8,64,128]{3,2,0,1:T(8,128)(2,1)S(1)}, u32[]{:S(2)}, u32[]{:S(2)}) async-start(bf16[2,8,64,128]{3,2,0,1:T(8,128)(2,1)} %copy.118), calls=%async_computation | async-start | bytes 524288 | tf_op jit(solution)/shard_map/all_to_all | solution.py:159
  33.6 3.6 %copy-start.6 = (bf16[2,8,64,128]{3,2,0,1:T(8,128)(2,1)}, bf16[2,8,64,128]{3,2,0,1:T(8,128)(2,1)S(1)}, u32[]{:S(2)}) copy-start(bf16[2,8,64,128]{3,2,0,1:T(8,128)(2,1)S(1)} %all-to-all-done) | copy-start | bytes 786436
  33.6 29.1 %all-to-all-start.2 = ((bf16[2,8,64,512]{3,2,0,1:T(8,128)(2,1)}), bf16[2,8,64,512]{3,2,0,1:T(8,128)(2,1)S(1)}, u32[]{:S(2)}, u32[]{:S(2)}) async-start(bf16[2,8,64,512]{3,2,0,1:T(8,128)(2,1)} %copy.127), calls=%async_computation.2 | async-start | bytes 2097152 | tf_op jit(solution)/shard_map/all_to_all | solution.py:153
  62.7 19.0 %copy-start.2 = (bf16[2,8,64,512]{3,2,0,1:T(8,128)(2,1)}, bf16[2,8,64,512]{3,2,0,1:T(8,128)(2,1)S(1)}, u32[]{:S(2)}) copy-start(bf16[2,8,64,512]{3,2,0,1:T(8,128)(2,1)S(1)} %all-to-all-done.2) | copy-start | bytes 3145732
  62.7 35.7 %all-to-all-start.4 = ((bf16[2,8,64,512]{3,2,0,1:T(8,128)(2,1)}), bf16[2,8,64,512]{3,2,0,1:T(8,128)(2,1)S(1)}, u32[]{:S(2)}, u32[]{:S(2)}) async-start(bf16[2,8,64,512]{3,2,0,1:T(8,128)(2,1)} %copy.134), calls=%async_computation.4 | async-start | bytes 2097152 | tf_op jit(solution)/shard_map/all_to_all | solution.py:162
  81.7 22.8 %collective-permute-start.1 = (bf16[1024,128]{1,0:T(8,128)(2,1)S(1)}, bf16[1024,128]{1,0:T(8,128)(2,1)}, u32[]{:S(2)}, u32[]{:S(2)}) collective-permute-start(bf16[1024,128]{1,0:T(8,128)(2,1)S(1)} %bitcast.127), channel_id=1, source_target_pairs={{0,8},{8,16},{16,24},{1,9},{9,17},{17,25},{2,10},{10,18},{18,26},{... | collective-permute-start | bytes 786440 | tf_op jit(solution)/shard_map/ppermute | solution.py:11
  86.2 66.5 %copy-start.1 = (pred[1024,2048]{0,1:T(8,128)(4,1)}, pred[1024,2048]{0,1:T(8,128)(4,1)S(1)}, u32[]{:S(2)}) copy-start(pred[1024,2048]{0,1:T(8,128)(4,1)S(1)} %compare_and_fusion) | copy-start | bytes 6291460
  89.9 62.8 %collective-permute-start = (bf16[1024,128]{0,1:T(8,128)(2,1)}, bf16[1024,128]{0,1:T(8,128)(2,1)}, u32[]{:S(2)}, u32[]{:S(2)}) collective-permute-start(bf16[1024,128]{0,1:T(8,128)(2,1)} %copy.121), channel_id=1, source_target_pairs={{0,8},{8,16},{16,24},{1,9},{9,17},{17,25},{2,10},{10,18},{18,26},{... | collective-permute-start | bytes 786440 | tf_op jit(solution)/shard_map/ppermute | solution.py:11
  104.5 48.2 %copy-start.3 = (bf16[1024,4,128]{0,2,1:T(8,128)(2,1)}, bf16[1024,4,128]{0,2,1:T(8,128)(2,1)S(1)}, u32[]{:S(2)}) copy-start(bf16[1024,4,128]{0,2,1:T(8,128)(2,1)S(1)} %reshape.537) | copy-start | bytes 3145732
  151.2 47.4 %collective-permute-start.3 = (f32[1024,128]{1,0:T(8,128)}, f32[1024,128]{1,0:T(8,128)}, u32[]{:S(2)}, u32[]{:S(2)}) collective-permute-start(f32[1024,128]{1,0:T(8,128)} %slice.39), channel_id=1, source_target_pairs={{8,0},{16,8},{24,16},{9,1},{17,9},{25,17},{10,2},{18,10},{26,18},{... | collective-permute-start | bytes 1572872 | tf_op jit(solution)/shard_map/ppermute | solution.py:11
  185.6 5.7 %copy-start = (bf16[4,1024,2048]{1,2,0:T(8,128)(2,1)}, bf16[4,1024,2048]{1,2,0:T(8,128)(2,1)S(1)}, u32[]{:S(2)}) copy-start(bf16[4,1024,2048]{1,2,0:T(8,128)(2,1)S(1)} %fusion.1) | copy-start | bytes 50331652
  197.3 1.4 copy-start.4
  197.3 9.2 %collective-permute-start.2 = (f32[1024,128]{1,0:T(8,128)S(1)}, f32[1024,128]{1,0:T(8,128)S(1)}, u32[]{:S(2)}, u32[]{:S(2)}) collective-permute-start(f32[1024,128]{1,0:T(8,128)S(1)} %slice.37), channel_id=1, source_target_pairs={{8,0},{16,8},{24,16},{9,1},{17,9},{25,17},{10,2},{18,10},{26,18},{... | collective-permute-start | bytes 1572872 | tf_op jit(solution)/shard_map/ppermute | solution.py:11
  200.6 15.4 %all-to-all-start.7 = ((bf16[2,8,64,128]{3,2,0,1:T(8,128)(2,1)}), bf16[2,8,64,128]{3,2,0,1:T(8,128)(2,1)S(1)}, u32[]{:S(2)}, u32[]{:S(2)}) async-start(bf16[2,8,64,128]{3,2,0,1:T(8,128)(2,1)} %copy.148), calls=%async_computation.7 | async-start | bytes 524288 | tf_op jit(solution)/shard_map/all_to_all | solution.py:214
  216.0 0.7 copy-start.7
  216.8 16.5 %all-to-all-start.6 = ((bf16[2,8,64,128]{3,2,0,1:T(8,128)(2,1)}), bf16[2,8,64,128]{3,2,0,1:T(8,128)(2,1)}, u32[]{:S(2)}, u32[]{:S(2)}) async-start(bf16[2,8,64,128]{3,2,0,1:T(8,128)(2,1)} %copy.145), calls=%async_computation.6 | async-start | bytes 524288 | tf_op jit(solution)/shard_map/all_to_all | solution.py:213
  233.3 31.9 %all-to-all-start.5 = ((bf16[2,8,64,512]{3,2,0,1:T(8,128)(2,1)}), bf16[2,8,64,512]{3,2,0,1:T(8,128)(2,1)S(1)}, u32[]{:S(2)}, u32[]{:S(2)}) async-start(bf16[2,8,64,512]{3,2,0,1:T(8,128)(2,1)} %copy.142), calls=%async_computation.5 | async-start | bytes 2097152 | tf_op jit(solution)/shard_map/all_to_all | solution.py:206
  265.2 29.6 %all-to-all-start.3 = ((bf16[2,8,64,512]{3,2,0,1:T(8,128)(2,1)}), bf16[2,8,64,512]{3,2,0,1:T(8,128)(2,1)S(1)}, u32[]{:S(2)}, u32[]{:S(2)}) async-start(bf16[2,8,64,512]{3,2,0,1:T(8,128)(2,1)} %copy.132), calls=%async_computation.3 | async-start | bytes 2097152 | tf_op jit(solution)/shard_map/all_to_all | solution.py:199
where the time goes:
time: 298 us; the launch traced here: 296 us
  waiting for transfers between devices  81.3 us (27%)
  matrix products  77.5 us (26%)
  local copies, waits for them, and re-layouts  53.7 us (18%)
  starting transfers between devices  47 us (16%)
  other arithmetic  23.4 us (8%)
  between operations  13.4 us (4%)
    all_to_all x1, waiting for transfers between devices, shards(): lax.all_to_all(pack_rows(query_rows, hold_index), 'inner', split_axis=1,...  20.7 us
    all_to_all x1, waiting for transfers between devices, shards(): lax.all_to_all(q_grads.reshape(2, n_inner, piece_len, width_q), 'inner',...  20.4 us
    all_to_all x1, waiting for transfers between devices, shards(): lax.all_to_all(attn.reshape(2, n_inner, piece_len, width_q), 'inner', spl...  20.1 us
    dot_general x1, matrix products, attend(): jnp.einsum('qhd,kd->hqk', g_three, value_buf, preferred_element_type=jnp....  16.5 us
    dot_general x1, matrix products, attend(): jnp.einsum('hqk,kd->qhd', probs_low, value_buf, preferred_element_type=jn...  16.4 us
    dot_general x1, matrix products, attend(): jnp.einsum('qhd,kd->hqk', q_three, key_buf, preferred_element_type=jnp.fl...  15.2 us
    dot_general x1, matrix products, attend(): jnp.einsum('hqk,qhd->kd', probs_low, g_three, preferred_element_type=jnp....  15.2 us
    reduce_sum x1, other arithmetic, attend(): jnp.sum(jnp.exp(scores - row_max), axis=2, keepdims=True)  14.3 us
  transfers between devices with their start and end apart: 12, of which 6 were waited for; matrix products, arithmetic and copies ran while one was open for 48% of the time, Pallas kernels for 0%

commit v1 on v0

--- a/solution.py
+++ b/solution.py
@@ -195,6 +195,24 @@
         .astype(jnp.bfloat16)
         .reshape(2, n_inner, piece_len, head_dim)
     )
+
+    def groups_handle(array_here):
+        v_now, b_next = (lax.axis_size("inner"), lax.axis_index("inner"))
+        after = array_here.shape[1] // v_now
+        aux = list(array_here.shape)
+        aux[1] = after
+        placed = aux[1]
+        aux[1] = placed * v_now
+        block_next = jnp.zeros(aux, array_here.dtype)
+        for ii in range(v_now):
+            part_next = lax.dynamic_slice_in_dim(array_here, (b_next ^ ii) * after, after, axis=1)
+            if ii:
+                part_next = lax.ppermute(part_next, "inner", [(p, p ^ ii) for p in range(v_now)])
+            block_next = lax.dynamic_update_slice_in_dim(
+                block_next, part_next, (b_next ^ ii) * placed, axis=1
+            )
+        return block_next
+
     attn_back, qg_back, kg_back, vg_back = (
         lax.all_to_all(
             attn.reshape(2, n_inner, piece_len, width_q),
@@ -203,13 +221,7 @@
             concat_axis=1,
             tiled=True,
         ),
-        lax.all_to_all(
-            q_grads.reshape(2, n_inner, piece_len, width_q),
-            "inner",
-            split_axis=1,
-            concat_axis=1,
-            tiled=True,
-        ),
+        groups_handle(q_grads.reshape(2, n_inner, piece_len, width_q)),
         lax.all_to_all(key_total, "inner", split_axis=1, concat_axis=1, tiled=True),
         lax.all_to_all(value_total, "inner", split_axis=1, concat_axis=1, tiled=True),
     )

time: 298 us -> 267 us (0.90)
  waiting for transfers between devices: 81.3 us -> 39.6 us
  starting transfers between devices: 47 us -> 59.9 us
  local copies, waits for them, and re-layouts: 53.7 us -> 49.3 us
    all_to_all x1, waiting for transfers between devices: 20.7 us -> 0.01 us  [shards(): lax.all_to_all(pack_rows(query_rows, hold_index), 'inner', split_axis=1,...]
    all_to_all x1 -> x0, waiting for transfers between devices: 20.4 us -> none  [shards(): lax.all_to_all(q_grads.reshape(2, n_inner, piece_len, width_q), 'inner',...]
    all_to_all x1, waiting for transfers between devices: 20.1 us -> 0.01 us  [shards(): lax.all_to_all(attn.reshape(2, n_inner, piece_len, width_q), 'inner', spl...]
    ppermute x0 -> x7, waiting for transfers between devices: none -> 18.4 us  [groups_handle(): lax.ppermute(part_next, 'inner', [(p, p ^ ii) for p in range(v_now)])]
    ppermute x0 -> x7, starting transfers between devices: none -> 15.9 us  [groups_handle(): lax.ppermute(part_next, 'inner', [(p, p ^ ii) for p in range(v_now)])]
    all_to_all x1 -> x0, starting transfers between devices: 6 us -> none  [shards(): lax.all_to_all(q_grads.reshape(2, n_inner, piece_len, width_q), 'inner',...]
    all_to_all x1, waiting for transfers between devices: 0.01 us -> 3.74 us  [shards(): lax.all_to_all(key_total, 'inner', split_axis=1, concat_axis=1, tiled=True)]
    another operation x2 -> x1, local copies, waits for them, and re-layouts: 3.86 us -> 0.44 us  [shards(): q_grads.reshape(2, n_inner, piece_len, width_q)]
  transfers between devices with their start and end apart: 12 -> 18, of which waited for: 6 -> 6; matrix products, arithmetic and copies ran while one was open for 48% -> 53% of each run, Pallas kernels for 0% -> 0%
where the time goes in v1:
time: 267 us; the launch traced here: 264 us
  matrix products  77.5 us (29%)
  starting transfers between devices  59.9 us (22%)
  local copies, waits for them, and re-layouts  49.3 us (18%)
  waiting for transfers between devices  39.6 us (15%)
  other arithmetic  24 us (9%)
  between operations  13.3 us (5%)
    ppermute x7, waiting for transfers between devices, groups_handle(): lax.ppermute(part_next, 'inner', [(p, p ^ ii) for p in range(v_now)])  18.4 us
    dot_general x1, matrix products, attend(): jnp.einsum('qhd,kd->hqk', g_three, value_buf, preferred_element_type=jnp....  16.5 us
    dot_general x1, matrix products, attend(): jnp.einsum('hqk,kd->qhd', probs_low, value_buf, preferred_element_type=jn...  16.3 us
    ppermute x7, starting transfers between devices, groups_handle(): lax.ppermute(part_next, 'inner', [(p, p ^ ii) for p in range(v_now)])  15.9 us
    dot_general x1, matrix products, attend(): jnp.einsum('hqk,qhd->kd', probs_low, g_three, preferred_element_type=jnp....  15.6 us
    dot_general x1, matrix products, attend(): jnp.einsum('qhd,kd->hqk', q_three, key_buf, preferred_element_type=jnp.fl...  14.9 us
    reduce_sum x1, other arithmetic, attend(): jnp.sum(jnp.exp(scores - row_max), axis=2, keepdims=True)  14.3 us
    ppermute x4, starting transfers between devices, passed_along(): return lax.ppermute(x, axis, pairs)  8.98 us
  transfers between devices with their start and end apart: 18, of which 6 were waited for; matrix products, arithmetic and copies ran while one was open for 53% of the time, Pallas kernels for 0%

profile of v1, /device:TPU:0, one launch (start us, length us, event | category | flops | bytes accessed | tf_op | source)
XLA Modules:
  0.0 263.6 jit_solution(9643104295429657010)
XLA Ops:
  5.2 7.3 %all-to-all-start.1 = ((bf16[2,8,64,128]{3,2,0,1:T(8,128)(2,1)}), bf16[2,8,64,128]{3,2,0,1:T(8,128)(2,1)S(1)}, u32[]{:S(2)}, u32[]{:S(2)}) async-start(bf16[2,8,64,128]{3,2,0,1:T(8,128)(2,1)} %copy.121), calls=%async_computation.1 | async-start | bytes 524288 | tf_op jit(solution)/shard_map/all_to_all | solution.py:156
  14.8 6.7 %all-to-all-done.1 = bf16[2,8,64,128]{3,2,0,1:T(8,128)(2,1)S(1)} async-done(((bf16[2,8,64,128]{3,2,0,1:T(8,128)(2,1)}), bf16[2,8,64,128]{3,2,0,1:T(8,128)(2,1)S(1)}, u32[]{:S(2)}, u32[]{:S(2)}) %all-to-all-start.1) | async-done | bytes 262176 | tf_op jit(solution)/shard_map/all_to_all | solution.py:156
  21.4 3.6 %all-to-all-start = ((bf16[2,8,64,128]{3,2,0,1:T(8,128)(2,1)}), bf16[2,8,64,128]{3,2,0,1:T(8,128)(2,1)S(1)}, u32[]{:S(2)}, u32[]{:S(2)}) async-start(bf16[2,8,64,128]{3,2,0,1:T(8,128)(2,1)} %copy.114), calls=%async_computation | async-start | bytes 524288 | tf_op jit(solution)/shard_map/all_to_all | solution.py:159
  30.5 3.1 %all-to-all-done = bf16[2,8,64,128]{3,2,0,1:T(8,128)(2,1)S(1)} async-done(((bf16[2,8,64,128]{3,2,0,1:T(8,128)(2,1)}), bf16[2,8,64,128]{3,2,0,1:T(8,128)(2,1)S(1)}, u32[]{:S(2)}, u32[]{:S(2)}) %all-to-all-start) | async-done | bytes 262176 | tf_op jit(solution)/shard_map/all_to_all | solution.py:159
  33.6 4.2 %all-to-all-start.2 = ((bf16[2,8,64,512]{3,2,0,1:T(8,128)(2,1)}), bf16[2,8,64,512]{3,2,0,1:T(8,128)(2,1)}, u32[]{:S(2)}, u32[]{:S(2)}) async-start(bf16[2,8,64,512]{3,2,0,1:T(8,128)(2,1)} %copy.123), calls=%async_computation.2 | async-start | bytes 2097152 | tf_op jit(solution)/shard_map/all_to_all | solution.py:153
  62.7 4.2 %collective-permute-start = (bf16[1024,128]{0,1:T(8,128)(2,1)}, bf16[1024,128]{0,1:T(8,128)(2,1)}, u32[]{:S(2)}, u32[]{:S(2)}) collective-permute-start(bf16[1024,128]{0,1:T(8,128)(2,1)} %copy.117), channel_id=1, source_target_pairs={{0,8},{8,16},{16,24},{1,9},{9,17},{17,25},{2,10},{10,18},{18,26},{... | collective-permute-start | bytes 786440 | tf_op jit(solution)/shard_map/ppermute | solution.py:11
  66.9 5.9 %all-to-all-start.4 = ((bf16[2,8,64,512]{3,2,0,1:T(8,128)(2,1)}), bf16[2,8,64,512]{3,2,0,1:T(8,128)(2,1)S(1)}, u32[]{:S(2)}, u32[]{:S(2)}) async-start(bf16[2,8,64,512]{3,2,0,1:T(8,128)(2,1)} %copy.130), calls=%async_computation.4 | async-start | bytes 2097152 | tf_op jit(solution)/shard_map/all_to_all | solution.py:162
  77.2 14.9 %fusion.3 = (f32[4,1024]{1,0:T(4,128)S(1)}, f32[2048,1024,4]{1,0,2:T(8,128)}) fusion(pred[1024,2048]{0,1:T(8,128)(4,1)S(1)} %compare_and_fusion, bf16[1024,4,128]{2,1,0:T(4,128)(2,1)} %reshape_reshape.12, bf16[1024,128]{1,0:T(8,128)(2,1)} %collective-permute-done.1, bf16[1024,128]{1,0:T(8,128)(2,1)S(1)} %bitcast.126), kind=kOutput, calls=%fused_computation.15 | convolution fusion | flops 2173693952 | bytes 37240832 | tf_op jit(solution)/shard_map/qhd,kd->hqk/dot_general | solution.py:93
  92.1 14.3 %exponential_reduce_fusion = f32[4,1024]{1,0:T(4,128)S(1)} fusion(f32[2048,1024,4]{1,0,2:T(8,128)} %get-tuple-element.52, f32[4,1024]{1,0:T(4,128)S(1)} %get-tuple-element.51, pred[1024,2048]{0,1:T(8,128)(4,1)S(1)} %compare_and_fusion), kind=kLoop, calls=%fused_computation.13 | loop fusion | flops 33550336 | bytes 35684352 | tf_op jit(solution)/shard_map/reduce_sum | solution.py:98
  109.4 3.2 %reshape.536 = bf16[1024,4,128]{0,2,1:T(8,128)(2,1)S(1)} reshape(bf16[2,8,64,512]{2,1,0,3:T(8,128)(2,1)} %copy.156) | data formatting | bytes 2097152 | tf_op jit(solution)/shard_map/reshape;reshape | solution.py:91
  112.6 15.6 %convolution_bitcast_fusion = f32[2048,128]{1,0:T(8,128)} fusion(bf16[1024,4,128]{0,2,1:T(8,128)(2,1)S(1)} %reshape.536, f32[2048,1024,4]{1,0,2:T(8,128)} %get-tuple-element.52, f32[4,1024]{1,0:T(4,128)S(1)} %log_add_fusion, pred[1024,2048]{0,1:T(8,128)(4,1)S(1)} %compare_and_fusion), kind=kOutput, calls=%fused_computation.17 | convolution fusion | flops 2181038080 | bytes 37765120 | tf_op jit(solution)/shard_map/hqk,qhd->kd/dot_general | solution.py:115
  131.6 16.3 %multiply_reduce_fusion = (f32[1024,4]{0,1:T(4,128)S(1)}, bf16[1024,4,128]{0,2,1:T(8,128)(2,1)}) fusion(bf16[1024,4,128]{0,2,1:T(8,128)(2,1)S(1)} %reshape.536, f32[2048,1024,4]{1,0,2:T(8,128)} %get-tuple-element.52, f32[4,1024]{1,0:T(4,128)S(1)} %log_add_fusion, pred[1024,2048]{0,1:T(8,128)(4,1)S(1)} %compare_and_fusion, ...), kind=kOutput, calls=%fused_computation.21 | convolution fusion | flops 2184704000 | bytes 38305792 | tf_op jit(solution)/shard_map/hqk,kd->qhd/dot_general | solution.py:101
  148.0 16.5 %fusion.1 = bf16[4,1024,2048]{1,2,0:T(8,128)(2,1)S(1)} fusion(f32[2048,1024,4]{1,0,2:T(8,128)} %get-tuple-element.52, bf16[1024,4,128]{0,2,1:T(8,128)(2,1)} %copy-done.2, f32[4,1024]{1,0:T(4,128)S(1)} %bitcast.150, f32[4,1024]{1,0:T(4,128)S(1)} %log_add_fusion, pred[1024,2048]{0,1:T(8,128)(4,1)} %copy-done.1, bf16[1024,128]{0,1:T(8,128)(2,1)} %collective-permute-done, ...), kind=kOutput, calls=%fused_computation.10 | convolution fusion | flops 2198863872 | bytes 54034432 | tf_op jit(solution)/shard_map/qhd,kd->hqk/dot_general | solution.py:105
  164.5 5.7 %copy-done = bf16[4,1024,2048]{1,2,0:T(8,128)(2,1)} copy-done((bf16[4,1024,2048]{1,2,0:T(8,128)(2,1)}, bf16[4,1024,2048]{1,2,0:T(8,128)(2,1)S(1)}, u32[]{:S(2)}) %copy-start) | copy-done | bytes 16777240
  170.2 6.0 %fusion.4 = f32[2048,128]{1,0:T(8,128)S(1)} fusion(bf16[4,1024,2048]{1,2,0:T(8,128)(2,1)S(1)} %fusion.1, bf16[1024,4,128]{2,1,0:T(4,128)(2,1)} %reshape_reshape.12), kind=kOutput, calls=%fused_computation.19 | convolution fusion | flops 2147745792 | bytes 18874368 | tf_op jit(solution)/shard_map/hqk,qhd->kd/dot_general | solution.py:112
  179.5 6.0 %all-to-all-start.6 = ((bf16[2,8,64,128]{3,2,0,1:T(8,128)(2,1)}), bf16[2,8,64,128]{3,2,0,1:T(8,128)(2,1)S(1)}, u32[]{:S(2)}, u32[]{:S(2)}) async-start(bf16[2,8,64,128]{3,2,0,1:T(8,128)(2,1)} %copy.142), calls=%async_computation.6 | async-start | bytes 524288 | tf_op jit(solution)/shard_map/all_to_all | solution.py:226
  187.3 7.6 %all-to-all-done.6 = bf16[2,8,64,128]{3,2,0,1:T(8,128)(2,1)S(1)} async-done(((bf16[2,8,64,128]{3,2,0,1:T(8,128)(2,1)}), bf16[2,8,64,128]{3,2,0,1:T(8,128)(2,1)S(1)}, u32[]{:S(2)}, u32[]{:S(2)}) %all-to-all-start.6) | async-done | bytes 262176 | tf_op jit(solution)/shard_map/all_to_all | solution.py:226
  195.0 4.4 %all-to-all-start.5 = ((bf16[2,8,64,128]{3,2,0,1:T(8,128)(2,1)}), bf16[2,8,64,128]{3,2,0,1:T(8,128)(2,1)S(1)}, u32[]{:S(2)}, u32[]{:S(2)}) async-start(bf16[2,8,64,128]{3,2,0,1:T(8,128)(2,1)} %copy.139), calls=%async_computation.5 | async-start | bytes 524288 | tf_op jit(solution)/shard_map/all_to_all | solution.py:225
  204.8 3.7 %all-to-all-done.5 = bf16[2,8,64,128]{3,2,0,1:T(8,128)(2,1)S(1)} async-done(((bf16[2,8,64,128]{3,2,0,1:T(8,128)(2,1)}), bf16[2,8,64,128]{3,2,0,1:T(8,128)(2,1)S(1)}, u32[]{:S(2)}, u32[]{:S(2)}) %all-to-all-start.5) | async-done | bytes 262176 | tf_op jit(solution)/shard_map/all_to_all | solution.py:225
  208.6 3.6 %all-to-all-start.3 = ((bf16[2,8,64,512]{3,2,0,1:T(8,128)(2,1)}), bf16[2,8,64,512]{3,2,0,1:T(8,128)(2,1)S(1)}, u32[]{:S(2)}, u32[]{:S(2)}) async-start(bf16[2,8,64,512]{3,2,0,1:T(8,128)(2,1)} %copy.128), calls=%async_computation.3 | async-start | bytes 2097152 | tf_op jit(solution)/shard_map/all_to_all | solution.py:217
  212.2 8.3 %fusion.6 = bf16[1024,4,128]{0,2,1:T(8,128)(2,1)S(1)} fusion(bf16[4,1024,2048]{1,2,0:T(8,128)(2,1)} %copy-done, bf16[1024,128]{1,0:T(8,128)(2,1)} %collective-permute-done.1, bf16[1024,128]{1,0:T(8,128)(2,1)S(1)} %bitcast.127), kind=kOutput, calls=%fused_computation.24 | convolution fusion | flops 2149580800 | bytes 18350080 | tf_op jit(solution)/shard_map/hqk,kd->qhd/dot_general | solution.py:108
  229.8 4.5 %collective-permute-start.7 = (bf16[2,1,64,512]{3,2,1,0:T(8,128)(2,1)S(1)}, bf16[2,1,64,512]{3,2,1,0:T(8,128)(2,1)S(1)}, u32[]{:S(2)}, u32[]{:S(2)}) collective-permute-start(bf16[2,1,64,512]{3,2,1,0:T(8,128)(2,1)S(1)} %get-tuple-element.36), channel_id=1, source_target_pairs={{0,6},{1,7},{2,4},{3,5},{4,2},{5,3},{6,0},{7,1},{8,14},{9,15},{10,... | collective-permute-start | bytes 393224 | tf_op jit(solution)/shard_map/ppermute | solution.py:210
  234.4 3.5 %collective-permute-start.8 = (bf16[2,1,64,512]{3,2,1,0:T(8,128)(2,1)S(1)}, bf16[2,1,64,512]{3,2,1,0:T(8,128)(2,1)S(1)}, u32[]{:S(2)}, u32[]{:S(2)}) collective-permute-start(bf16[2,1,64,512]{3,2,1,0:T(8,128)(2,1)S(1)} %get-tuple-element.35), channel_id=1, source_target_pairs={{0,7},{1,6},{2,5},{3,4},{4,3},{5,2},{6,1},{7,0},{8,15},{9,14},{10,... | collective-permute-start | bytes 393224 | tf_op jit(solution)/shard_map/ppermute | solution.py:210
  237.9 15.5 %collective-permute-done.5 = bf16[2,1,64,512]{3,2,1,0:T(8,128)(2,1)S(1)} collective-permute-done((bf16[2,1,64,512]{3,2,1,0:T(8,128)(2,1)S(1)}, bf16[2,1,64,512]{3,2,1,0:T(8,128)(2,1)S(1)}, u32[]{:S(2)}, u32[]{:S(2)}) %collective-permute-start.5) | collective-permute-done | bytes 131104 | tf_op jit(solution)/shard_map/ppermute | solution.py:210
  (116 shorter events, 65.7 us)
Async XLA Ops:
  5.2 16.2 %all-to-all-start.1 = ((bf16[2,8,64,128]{3,2,0,1:T(8,128)(2,1)}), bf16[2,8,64,128]{3,2,0,1:T(8,128)(2,1)S(1)}, u32[]{:S(2)}, u32[]{:S(2)}) async-start(bf16[2,8,64,128]{3,2,0,1:T(8,128)(2,1)} %copy.121), calls=%async_computation.1 | async-start | bytes 524288 | tf_op jit(solution)/shard_map/all_to_all | solution.py:156
  21.4 12.2 %all-to-all-start = ((bf16[2,8,64,128]{3,2,0,1:T(8,128)(2,1)}), bf16[2,8,64,128]{3,2,0,1:T(8,128)(2,1)S(1)}, u32[]{:S(2)}, u32[]{:S(2)}) async-start(bf16[2,8,64,128]{3,2,0,1:T(8,128)(2,1)} %copy.114), calls=%async_computation | async-start | bytes 524288 | tf_op jit(solution)/shard_map/all_to_all | solution.py:159
  33.6 33.3 %all-to-all-start.2 = ((bf16[2,8,64,512]{3,2,0,1:T(8,128)(2,1)}), bf16[2,8,64,512]{3,2,0,1:T(8,128)(2,1)}, u32[]{:S(2)}, u32[]{:S(2)}) async-start(bf16[2,8,64,512]{3,2,0,1:T(8,128)(2,1)} %copy.123), calls=%async_computation.2 | async-start | bytes 2097152 | tf_op jit(solution)/shard_map/all_to_all | solution.py:153
  52.1 25.1 %collective-permute-start.1 = (bf16[1024,128]{1,0:T(8,128)(2,1)S(1)}, bf16[1024,128]{1,0:T(8,128)(2,1)}, u32[]{:S(2)}, u32[]{:S(2)}) collective-permute-start(bf16[1024,128]{1,0:T(8,128)(2,1)S(1)} %bitcast.125), channel_id=1, source_target_pairs={{0,8},{8,16},{16,24},{1,9},{9,17},{17,25},{2,10},{10,18},{18,26},{... | collective-permute-start | bytes 786440 | tf_op jit(solution)/shard_map/ppermute | solution.py:11
  56.4 75.2 %copy-start.1 = (pred[1024,2048]{0,1:T(8,128)(4,1)}, pred[1024,2048]{0,1:T(8,128)(4,1)S(1)}, u32[]{:S(2)}) copy-start(pred[1024,2048]{0,1:T(8,128)(4,1)S(1)} %compare_and_fusion) | copy-start | bytes 6291460
  62.7 68.9 %collective-permute-start = (bf16[1024,128]{0,1:T(8,128)(2,1)}, bf16[1024,128]{0,1:T(8,128)(2,1)}, u32[]{:S(2)}, u32[]{:S(2)}) collective-permute-start(bf16[1024,128]{0,1:T(8,128)(2,1)} %copy.117), channel_id=1, source_target_pairs={{0,8},{8,16},{16,24},{1,9},{9,17},{17,25},{2,10},{10,18},{18,26},{... | collective-permute-start | bytes 786440 | tf_op jit(solution)/shard_map/ppermute | solution.py:11
  66.9 39.6 %all-to-all-start.4 = ((bf16[2,8,64,512]{3,2,0,1:T(8,128)(2,1)}), bf16[2,8,64,512]{3,2,0,1:T(8,128)(2,1)S(1)}, u32[]{:S(2)}, u32[]{:S(2)}) async-start(bf16[2,8,64,512]{3,2,0,1:T(8,128)(2,1)} %copy.130), calls=%async_computation.4 | async-start | bytes 2097152 | tf_op jit(solution)/shard_map/all_to_all | solution.py:162
  112.6 19.0 %copy-start.2 = (bf16[1024,4,128]{0,2,1:T(8,128)(2,1)}, bf16[1024,4,128]{0,2,1:T(8,128)(2,1)S(1)}, u32[]{:S(2)}) copy-start(bf16[1024,4,128]{0,2,1:T(8,128)(2,1)S(1)} %reshape.536) | copy-start | bytes 3145732
  130.1 47.4 %collective-permute-start.10 = (f32[1024,128]{1,0:T(8,128)}, f32[1024,128]{1,0:T(8,128)}, u32[]{:S(2)}, u32[]{:S(2)}) collective-permute-start(f32[1024,128]{1,0:T(8,128)} %slice.39), channel_id=1, source_target_pairs={{8,0},{16,8},{24,16},{9,1},{17,9},{25,17},{10,2},{18,10},{26,18},{... | collective-permute-start | bytes 1572872 | tf_op jit(solution)/shard_map/ppermute | solution.py:11
  164.4 5.7 %copy-start = (bf16[4,1024,2048]{1,2,0:T(8,128)(2,1)}, bf16[4,1024,2048]{1,2,0:T(8,128)(2,1)S(1)}, u32[]{:S(2)}) copy-start(bf16[4,1024,2048]{1,2,0:T(8,128)(2,1)S(1)} %fusion.1) | copy-start | bytes 50331652
  176.1 1.4 copy-start.3
  176.2 9.3 %collective-permute-start.9 = (f32[1024,128]{1,0:T(8,128)S(1)}, f32[1024,128]{1,0:T(8,128)S(1)}, u32[]{:S(2)}, u32[]{:S(2)}) collective-permute-start(f32[1024,128]{1,0:T(8,128)S(1)} %slice.37), channel_id=1, source_target_pairs={{8,0},{16,8},{24,16},{9,1},{17,9},{25,17},{10,2},{18,10},{26,18},{... | collective-permute-start | bytes 1572872 | tf_op jit(solution)/shard_map/ppermute | solution.py:11
  179.5 15.5 %all-to-all-start.6 = ((bf16[2,8,64,128]{3,2,0,1:T(8,128)(2,1)}), bf16[2,8,64,128]{3,2,0,1:T(8,128)(2,1)S(1)}, u32[]{:S(2)}, u32[]{:S(2)}) async-start(bf16[2,8,64,128]{3,2,0,1:T(8,128)(2,1)} %copy.142), calls=%async_computation.6 | async-start | bytes 524288 | tf_op jit(solution)/shard_map/all_to_all | solution.py:226
  195.0 4.4 %copy-start.4 = (bf16[2,8,64,128]{3,2,0,1:T(8,128)(2,1)}, bf16[2,8,64,128]{3,2,0,1:T(8,128)(2,1)S(1)}, u32[]{:S(2)}) copy-start(bf16[2,8,64,128]{3,2,0,1:T(8,128)(2,1)S(1)} %all-to-all-done.6) | copy-start | bytes 786436
  195.0 13.6 %all-to-all-start.5 = ((bf16[2,8,64,128]{3,2,0,1:T(8,128)(2,1)}), bf16[2,8,64,128]{3,2,0,1:T(8,128)(2,1)S(1)}, u32[]{:S(2)}, u32[]{:S(2)}) async-start(bf16[2,8,64,128]{3,2,0,1:T(8,128)(2,1)} %copy.139), calls=%async_computation.5 | async-start | bytes 524288 | tf_op jit(solution)/shard_map/all_to_all | solution.py:225
  208.6 3.6 %copy-start.5 = (bf16[2,8,64,128]{3,2,0,1:T(8,128)(2,1)}, bf16[2,8,64,128]{3,2,0,1:T(8,128)(2,1)S(1)}, u32[]{:S(2)}) copy-start(bf16[2,8,64,128]{3,2,0,1:T(8,128)(2,1)S(1)} %all-to-all-done.5) | copy-start | bytes 786436
  208.6 53.5 %all-to-all-start.3 = ((bf16[2,8,64,512]{3,2,0,1:T(8,128)(2,1)}), bf16[2,8,64,512]{3,2,0,1:T(8,128)(2,1)S(1)}, u32[]{:S(2)}, u32[]{:S(2)}) async-start(bf16[2,8,64,512]{3,2,0,1:T(8,128)(2,1)} %copy.128), calls=%async_computation.3 | async-start | bytes 2097152 | tf_op jit(solution)/shard_map/all_to_all | solution.py:217
  221.9 7.9 %collective-permute-start.2 = (bf16[2,1,64,512]{3,2,1,0:T(8,128)(2,1)S(1)}, bf16[2,1,64,512]{3,2,1,0:T(8,128)(2,1)S(1)}, u32[]{:S(2)}, u32[]{:S(2)}) collective-permute-start(bf16[2,1,64,512]{3,2,1,0:T(8,128)(2,1)S(1)} %get-tuple-element.41), channel_id=1, source_target_pairs={{0,1},{1,0},{2,3},{3,2},{4,5},{5,4},{6,7},{7,6},{8,9},{9,8},{10,11... | collective-permute-start | bytes 393224 | tf_op jit(solution)/shard_map/ppermute | solution.py:210
  224.0 10.4 %collective-permute-start.3 = (bf16[2,1,64,512]{3,2,1,0:T(8,128)(2,1)S(1)}, bf16[2,1,64,512]{3,2,1,0:T(8,128)(2,1)S(1)}, u32[]{:S(2)}, u32[]{:S(2)}) collective-permute-start(bf16[2,1,64,512]{3,2,1,0:T(8,128)(2,1)S(1)} %get-tuple-element.40), channel_id=1, source_target_pairs={{0,2},{1,3},{2,0},{3,1},{4,6},{5,7},{6,4},{7,5},{8,10},{9,11},{10,... | collective-permute-start | bytes 393224 | tf_op jit(solution)/shard_map/ppermute | solution.py:210
  225.4 12.4 %collective-permute-start.4 = (bf16[2,1,64,512]{3,2,1,0:T(8,128)(2,1)S(1)}, bf16[2,1,64,512]{3,2,1,0:T(8,128)(2,1)S(1)}, u32[]{:S(2)}, u32[]{:S(2)}) collective-permute-start(bf16[2,1,64,512]{3,2,1,0:T(8,128)(2,1)S(1)} %get-tuple-element.39), channel_id=1, source_target_pairs={{0,3},{1,2},{2,1},{3,0},{4,7},{5,6},{6,5},{7,4},{8,11},{9,10},{10,... | collective-permute-start | bytes 393224 | tf_op jit(solution)/shard_map/ppermute | solution.py:210
  225.5 27.8 %collective-permute-start.5 = (bf16[2,1,64,512]{3,2,1,0:T(8,128)(2,1)S(1)}, bf16[2,1,64,512]{3,2,1,0:T(8,128)(2,1)S(1)}, u32[]{:S(2)}, u32[]{:S(2)}) collective-permute-start(bf16[2,1,64,512]{3,2,1,0:T(8,128)(2,1)S(1)} %get-tuple-element.38), channel_id=1, source_target_pairs={{0,4},{1,5},{2,6},{3,7},{4,0},{5,1},{6,2},{7,3},{8,12},{9,13},{10,... | collective-permute-start | bytes 393224 | tf_op jit(solution)/shard_map/ppermute | solution.py:210
  228.4 27.9 %collective-permute-start.6 = (bf16[2,1,64,512]{3,2,1,0:T(8,128)(2,1)S(1)}, bf16[2,1,64,512]{3,2,1,0:T(8,128)(2,1)S(1)}, u32[]{:S(2)}, u32[]{:S(2)}) collective-permute-start(bf16[2,1,64,512]{3,2,1,0:T(8,128)(2,1)S(1)} %get-tuple-element.37), channel_id=1, source_target_pairs={{0,5},{1,4},{2,7},{3,6},{4,1},{5,0},{6,3},{7,2},{8,13},{9,12},{10,... | collective-permute-start | bytes 393224 | tf_op jit(solution)/shard_map/ppermute | solution.py:210
  229.8 26.5 %collective-permute-start.7 = (bf16[2,1,64,512]{3,2,1,0:T(8,128)(2,1)S(1)}, bf16[2,1,64,512]{3,2,1,0:T(8,128)(2,1)S(1)}, u32[]{:S(2)}, u32[]{:S(2)}) collective-permute-start(bf16[2,1,64,512]{3,2,1,0:T(8,128)(2,1)S(1)} %get-tuple-element.36), channel_id=1, source_target_pairs={{0,6},{1,7},{2,4},{3,5},{4,2},{5,3},{6,0},{7,1},{8,14},{9,15},{10,... | collective-permute-start | bytes 393224 | tf_op jit(solution)/shard_map/ppermute | solution.py:210
  234.4 22.0 %collective-permute-start.8 = (bf16[2,1,64,512]{3,2,1,0:T(8,128)(2,1)S(1)}, bf16[2,1,64,512]{3,2,1,0:T(8,128)(2,1)S(1)}, u32[]{:S(2)}, u32[]{:S(2)}) collective-permute-start(bf16[2,1,64,512]{3,2,1,0:T(8,128)(2,1)S(1)} %get-tuple-element.35), channel_id=1, source_target_pairs={{0,7},{1,6},{2,5},{3,4},{4,3},{5,2},{6,1},{7,0},{8,15},{9,14},{10,... | collective-permute-start | bytes 393224 | tf_op jit(solution)/shard_map/ppermute | solution.py:210
